TPU v7x, 32 devices: a whole 2x2x4 slice. The times are simulated.
32 devices in a mesh: frames: 2 (over x), lenslet: 16 (over z, y, core).
Axes of the slice: x: 2, y: 2, z: 4, core: 2. Of those that a mesh axis runs over, the one named last changes fastest.
Arguments:
- volume: bfloat16 [8, 256, 64, 400], P('frames', 'lenslet'), parts along dimension 0, may hold values from 0.099609375 to 1
- measured: float32 [512, 64, 400], P(('frames', 'lenslet')), parts along dimension 0, may hold values from 0.2 to 2
- operator_rows: bfloat16 [12800, 400], P('lenslet'), may hold values from 2.9831426e-10 to 0.0029907227
- offset_counts: int32 [4], replicated, may hold values from 1 to 25, 32 in all
- offset_table: int32 [32, 2], replicated, may hold values from -2 to 2
- dark_level: float32 [400], replicated, may hold values from 0.2 to 1
Outputs:
- predicted: float32 [512, 64, 400], P(('frames', 'lenslet')), parts along dimension 0
- ratio: float32 [512, 64, 400], P(('frames', 'lenslet')), parts along dimension 0
There are 2 independent parts, one for each index of `frames`. A program takes and returns all parts, laid end to end along the dimension named above; an argument that names none is the same for every part. Nothing has to cross between parts.
Inputs may be any that keep to these rules, and one draw needn't show every extreme that they name: `offset_counts`: counts sum to 32.
All inputs are finite; a program needn't handle non-finite values.
Results may differ from a plain program's by a relative error of at most 0.0003.
Values may be sent and summed in bfloat16 or wider, within the bound.
No kernel may reach another device: no remote copies, remote signals or barrier semaphores. Data moves between devices by JAX's collectives and lax.ppermute only.
A program may use at most 192 MiB of HBM per device.

v0:
```python
import jax
import jax.numpy as jnp
from jax import lax
from jax.sharding import PartitionSpec as P

REACH = 2


def passed_along(block, axis, distance):
    devices = range(lax.axis_size(axis))
    route = [(i - distance, i) for i in devices if i - distance in devices]
    return lax.ppermute(block, axis, route)


def gather_slabs(table, depth_of, row_start, col_shift, target_rows, columns, rows_ext, cols_ext):
    row_ids = jnp.arange(target_rows, dtype=jnp.int32)
    col_ids = jnp.arange(columns, dtype=jnp.int32)
    index = depth_of[None, None, :] * (rows_ext * cols_ext)
    index = index + (row_ids[:, None, None] + row_start[None, None, :]) * cols_ext
    index = index + col_ids[None, :, None] + col_shift[None, None, :] + REACH
    pixels = table.shape[1]
    taken = jnp.take(table, index.reshape(-1), axis=0)
    return taken.reshape(target_rows * columns, depth_of.shape[0] * pixels)


def body(volume, measured, operator_rows, offset_counts, offset_table, dark_level):
    depths, rows_here, columns, pixels = volume.shape
    op_total = offset_table.shape[0]
    ends = jnp.cumsum(offset_counts)
    positions = jnp.arange(op_total, dtype=jnp.int32)
    depth_of = jnp.sum((positions[:, None] >= ends[None, :]).astype(jnp.int32), axis=1)
    row_shift = offset_table[:, 0]
    col_shift = offset_table[:, 1]
    cols_ext = columns + 2 * REACH
    above = passed_along(volume[:, rows_here - REACH :], "lenslet", 1)
    below = passed_along(volume[:, :REACH], "lenslet", -1)
    extended = jnp.concatenate([above, volume, below], axis=1)
    extended = jnp.pad(extended, ((0, 0), (0, 0), (REACH, REACH), (0, 0)))
    rows_ext = rows_here + 2 * REACH
    table = extended.reshape(depths * rows_ext * cols_ext, pixels)
    stacked = gather_slabs(
        table, depth_of, row_shift + REACH, col_shift, rows_here, columns, rows_ext, cols_ext
    )
    summed = jnp.dot(
        stacked,
        lax.all_gather(operator_rows, "lenslet", axis=0, tiled=True),
        preferred_element_type=jnp.float32,
    )
    predicted = summed.reshape(rows_here, columns, pixels)
    ratio = measured / (predicted + dark_level)
    return (predicted, ratio)


def solution(mesh):
    placed = (
        P("frames", "lenslet", None, None),
        P(("frames", "lenslet"), None, None),
        P("lenslet", None),
        P(),
        P(),
        P(),
    )
    return jax.shard_map(
        body,
        mesh=mesh,
        in_specs=placed,
        out_specs=(P(("frames", "lenslet"), None, None), P(("frames", "lenslet"), None, None)),
        check_vma=False,
    )
```

profile of v0, /device:TPU:1, one launch (start us, length us, event | category | flops | bytes accessed | tf_op | source)
XLA Modules:
  0.0 349.6 jit_solution(12887176921181222401)
XLA Ops:
  7.2 0.0 all-gather.3.cloned.1.call-start
  7.2 0.7 all-gather.3.cloned.1.call-update
  7.9 2.1 fusion.10
  10.0 4.5 %collective-permute-start = (bf16[4,2,64,400]{3,2,1,0:T(8,128)(2,1)}, bf16[4,2,64,400]{3,2,1,0:T(8,128)(2,1)S(1)}, u32[]{:S(2)}, u32[]{:S(2)}) collective-permute-start(bf16[4,2,64,400]{3,2,1,0:T(8,128)(2,1)} %get-tuple-element.2), channel_id=1, source_target_pairs={{0,1},{1,2},{2,3},{3,4},{4,5},{5,6},{6,7},{7,8},{8,9},{9,10},{10,1... | collective-permute-start | bytes 1228808 | tf_op jit(solution)/shard_map/ppermute | solution.py:12
  14.5 1.9 collective-permute-start.1
  16.5 0.8 reduce-window.8
  17.3 0.1 convert_reduce_fusion
  17.4 0.8 slice_bitcast_fusion
  18.1 0.2 add_add_fusion.1
  18.3 0.3 add.184
  18.6 0.3 add.187
  18.9 0.2 compare_select_fusion.1
  19.1 0.2 compare_and_fusion
  19.3 6.8 %broadcast_in_dim.12 = pred[1024,32,400]{2,1,0:T(32,128)(4,1)} broadcast(pred[1024,32]{1,0:T(8,128)(4,1)S(1)} %compare_and_fusion), dimensions={0,1} | broadcast | bytes 13139968 | tf_op jit(solution)/shard_map/jit(_take)/broadcast_in_dim | solution.py:22
  26.0 53.5 %broadcast_in_dim.20 = pred[16,64,12800]{2,1,0:T(32,128)(4,1)} reshape(pred[1024,32,400]{2,1,0:T(32,128)(4,1)} %broadcast_in_dim.12) | data formatting | bytes 26214400 | tf_op jit(solution)/shard_map/jit(_take)/broadcast_in_dim | solution.py:22
  79.5 0.0 collective-permute-done
  79.5 0.0 collective-permute-done.1
  79.5 8.0 %fusion.8 = bf16[4,20,68,400]{3,2,1,0:T(8,128)(2,1)} fusion(bf16[4,2,64,400]{3,2,1,0:T(8,128)(2,1)S(1)} %collective-permute-done.1, bf16[4,16,64,400]{3,2,1,0:T(8,128)(2,1)} %param.6, bf16[4,2,64,400]{3,2,1,0:T(8,128)(2,1)S(1)} %collective-permute-done), kind=kLoop, calls=%fused_computation.11 | loop fusion | flops 26112000 | bytes 8448000 | tf_op jit(solution)/shard_map/concatenate | solution.py:37
  87.6 9.2 %reshape.157 = bf16[5440,400]{1,0:T(8,128)(2,1)} reshape(bf16[4,20,68,400]{3,2,1,0:T(8,128)(2,1)} %fusion.8) | data formatting | bytes 8704000 | tf_op jit(solution)/shard_map/reshape | solution.py:40
  96.8 135.6 %gather_fusion = bf16[32768,400]{1,0:T(8,128)(2,1)} fusion(bf16[5440,400]{1,0:T(8,128)(2,1)} %reshape.157, s32[32768]{0:T(1024)S(1)} %broadcast_clamp_fusion), kind=kCustom, calls=%fused_computation | custom fusion | bytes 52559872 | tf_op jit(solution)/shard_map/jit(_take)/gather | solution.py:22
  232.4 52.4 %gather.7 = bf16[16,64,12800]{2,1,0:T(8,128)(2,1)} reshape(bf16[32768,400]{1,0:T(8,128)(2,1)} %gather_fusion) | data formatting | bytes 52428800 | tf_op jit(solution)/shard_map/jit(_take)/gather | solution.py:22
  284.8 0.0 all-gather.3.cloned.1.call-done
  284.8 16.2 %copy.11 = bf16[16,800,400]{1,0,2:T(8,128)(2,1)} copy(bf16[16,800,400]{1,2,0:T(8,128)(2,1)} %all-gather.3.cloned.1.call-done) | data formatting | bytes 20480000 | tf_op jit(solution)/shard_map/all_gather | solution.py:46
  300.9 0.0 copy-start
  301.0 0.0 copy-start.1
  301.0 18.7 %reshape.168 = bf16[12800,400,1]{0,1,2:T(8,128)(2,1)} reshape(bf16[16,800,400]{1,0,2:T(8,128)(2,1)} %copy.11) | data formatting | bytes 20480000
  319.7 0.0 copy-done
  319.7 0.0 copy-done.1
  319.7 23.0 %add_divide_fusion = (f32[16,64,400]{2,1,0:T(8,128)}, f32[16,64,400]{2,1,0:T(8,128)}) fusion(f32[16,64,400]{2,1,0:T(8,128)S(1)} %copy-done, f32[400]{0:T(512)S(1)} %copy-done.1, bf16[12800,400,1]{0,1,2:T(8,128)(2,1)} %reshape.168, pred[16,64,12800]{2,1,0:T(32,128)(4,1)} %broadcast_in_dim.20, bf16[16,64,12800]{2,1,0:T(8,128)(2,1)} %gather.7), kind=kOutput, calls=%fused_computation.12 | convolution fusion | flops 10499686400 | bytes 54478400 | tf_op jit(solution)/shard_map/dot_general | solution.py:44
  (3 shorter events, 0.0 us)
Async XLA Ops:
  7.2 277.6 %all-gather.3.cloned.1.call-start = ((), (), s32[]{:S(2)}) async-start(), calls=%async_computation | async-start | bytes 12185600 | tf_op jit(solution)/shard_map/all_gather | solution.py:46
  10.0 69.5 %collective-permute-start = (bf16[4,2,64,400]{3,2,1,0:T(8,128)(2,1)}, bf16[4,2,64,400]{3,2,1,0:T(8,128)(2,1)S(1)}, u32[]{:S(2)}, u32[]{:S(2)}) collective-permute-start(bf16[4,2,64,400]{3,2,1,0:T(8,128)(2,1)} %get-tuple-element.2), channel_id=1, source_target_pairs={{0,1},{1,2},{2,3},{3,4},{4,5},{5,6},{6,7},{7,8},{8,9},{9,10},{10,1... | collective-permute-start | bytes 1228808 | tf_op jit(solution)/shard_map/ppermute | solution.py:12
  14.5 65.0 %collective-permute-start.1 = (bf16[4,2,64,400]{3,2,1,0:T(8,128)(2,1)S(1)}, bf16[4,2,64,400]{3,2,1,0:T(8,128)(2,1)S(1)}, u32[]{:S(2)}, u32[]{:S(2)}) collective-permute-start(bf16[4,2,64,400]{3,2,1,0:T(8,128)(2,1)S(1)} %get-tuple-element.3), channel_id=1, source_target_pairs={{1,0},{2,1},{3,2},{4,3},{5,4},{6,5},{7,6},{8,7},{9,8},{10,9},{11,1... | collective-permute-start | bytes 1228808 | tf_op jit(solution)/shard_map/ppermute | solution.py:12
  300.9 18.7 %copy-start = (f32[16,64,400]{2,1,0:T(8,128)S(1)}, f32[16,64,400]{2,1,0:T(8,128)}, u32[]{:S(2)}) copy-start(f32[16,64,400]{2,1,0:T(8,128)} %param.7) | copy-start | bytes 4915204
  301.0 18.7 %copy-start.1 = (f32[400]{0:T(512)S(1)}, f32[400]{0:T(512)}, u32[]{:S(2)}) copy-start(f32[400]{0:T(512)} %param.11) | copy-start | bytes 4804
Sparse Core Ops, SparseCore 0:
  10.2 98.2 all-gather.2
where the time goes:
time: 352 us; the launch traced here: 350 us
  local copies, waits for them, and re-layouts  295 us (84%)
  matrix products  23 us (7%)
  between operations  14.1 us (4%)
  other arithmetic  10.3 us (3%)
  starting transfers between devices  6.48 us (2%)
    gather x2, local copies, waits for them, and re-layouts, gather_slabs(): taken = jnp.take(table, index.reshape(-1), axis=0)  188 us
    broadcast_in_dim x2, local copies, waits for them, and re-layouts, gather_slabs(): taken = jnp.take(table, index.reshape(-1), axis=0)  60.3 us
    dot_general x1, matrix products, body(): jnp.dot(stacked, lax.all_gather(operator_rows, 'lenslet', axis=0, tiled=T...  23 us
    unnamed x5, local copies, waits for them, and re-layouts  18.7 us
    all_gather x1, local copies, waits for them, and re-layouts, body(): lax.all_gather(operator_rows, 'lenslet', axis=0, tiled=True)  16.2 us
    reshape x1, local copies, waits for them, and re-layouts, body(): table = extended.reshape(depths * rows_ext * cols_ext, pixels)  9.23 us
    concatenate x1, other arithmetic, body(): extended = jnp.concatenate([above, volume, below], axis=1)  8.03 us
  transfers between devices with their start and end apart: 3, of which 0 were waited for; matrix products, arithmetic and copies ran while one was open for 77% of the time, Pallas kernels for 0%

commit v1 on v0

v1 whole, which is shorter than its diff:
```python
import jax
import jax.numpy as jnp
from jax import lax
from jax.experimental import pallas as pl
from jax.experimental.pallas import tpu as pltpu
from jax.sharding import PartitionSpec as P

REACH = 2


def passed_along(block, axis, distance):
    devices = range(lax.axis_size(axis))
    route = [(i - distance, i) for i in devices if i - distance in devices]
    return lax.ppermute(block, axis, route)


def project_kernel(depth_ref, row_ref, col_ref, vol_ref, op_ref, meas_ref, dark_ref, pred_ref, ratio_ref):
    k = pl.program_id(0)
    _, _, _, columns, pixels = vol_ref.shape
    rows = pred_ref.shape[0] // columns

    @pl.when(k == 0)
    def _():
        pred_ref[...] = jnp.zeros_like(pred_ref)

    slab = vol_ref[col_ref[k], depth_ref[k], pl.ds(row_ref[k], rows), :, :]
    slab = slab.reshape(rows * columns, pixels)
    pred_ref[...] += jnp.dot(slab, op_ref[...], preferred_element_type=jnp.float32)

    @pl.when(k == pl.num_programs(0) - 1)
    def _():
        ratio_ref[...] = meas_ref[...] / (pred_ref[...] + dark_ref[...])


def body(volume, measured, operator_rows, offset_counts, offset_table, dark_level):
    depths, rows_here, columns, pixels = volume.shape
    op_total = offset_table.shape[0]
    ends = jnp.cumsum(offset_counts)
    positions = jnp.arange(op_total, dtype=jnp.int32)
    depth_of = jnp.sum((positions[:, None] >= ends[None, :]).astype(jnp.int32), axis=1)
    row_start = (offset_table[:, 0] + REACH).astype(jnp.int32)
    col_start = (offset_table[:, 1] + REACH).astype(jnp.int32)
    above = passed_along(volume[:, rows_here - REACH :], "lenslet", 1)
    below = passed_along(volume[:, :REACH], "lenslet", -1)
    extended = jnp.concatenate([above, volume, below], axis=1)
    extended = jnp.pad(extended, ((0, 0), (0, 0), (REACH, REACH), (0, 0)))
    shifted = jnp.stack([extended[:, :, s : s + columns] for s in range(2 * REACH + 1)])
    operators = lax.all_gather(operator_rows, "lenslet", axis=0, tiled=True)
    image_rows = rows_here * columns
    flat = lambda k, *_: (0, 0)
    predicted, ratio = pl.pallas_call(
        project_kernel,
        grid_spec=pltpu.PrefetchScalarGridSpec(
            num_scalar_prefetch=3,
            grid=(op_total,),
            in_specs=[
                pl.BlockSpec(memory_space=pltpu.VMEM),
                pl.BlockSpec((pixels, pixels), lambda k, *_: (k, 0)),
                pl.BlockSpec((image_rows, pixels), flat),
                pl.BlockSpec((1, pixels), flat),
            ],
            out_specs=[
                pl.BlockSpec((image_rows, pixels), flat),
                pl.BlockSpec((image_rows, pixels), flat),
            ],
        ),
        out_shape=[
            jax.ShapeDtypeStruct((image_rows, pixels), jnp.float32),
            jax.ShapeDtypeStruct((image_rows, pixels), jnp.float32),
        ],
        compiler_params=pltpu.CompilerParams(dimension_semantics=("arbitrary",)),
    )(
        depth_of,
        row_start,
        col_start,
        shifted,
        operators,
        measured.reshape(image_rows, pixels),
        dark_level.reshape(1, pixels),
    )
    return (predicted.reshape(rows_here, columns, pixels), ratio.reshape(rows_here, columns, pixels))


def solution(mesh):
    placed = (
        P("frames", "lenslet", None, None),
        P(("frames", "lenslet"), None, None),
        P("lenslet", None),
        P(),
        P(),
        P(),
    )
    return jax.shard_map(
        body,
        mesh=mesh,
        in_specs=placed,
        out_specs=(P(("frames", "lenslet"), None, None), P(("frames", "lenslet"), None, None)),
        check_vma=False,
    )
```

time: 352 us -> 172 us (0.49)
  local copies, waits for them, and re-layouts: 295 us -> 43.3 us
  waiting for transfers between devices: 0.69 us -> 63.6 us
  Pallas kernels: 0 us -> 40.1 us
  matrix products: 23 us -> 0 us
  other arithmetic: 10.3 us -> 2.79 us
    gather x2 -> x0, local copies, waits for them, and re-layouts: 188 us -> none  [gather_slabs(): taken = jnp.take(table, index.reshape(-1), axis=0)]
    broadcast_in_dim x2 -> x0, local copies, waits for them, and re-layouts: 60.3 us -> none  [gather_slabs(): taken = jnp.take(table, index.reshape(-1), axis=0)]
    all_gather x1, waiting for transfers between devices: 0.01 us -> 55.6 us  [body(): operators = lax.all_gather(operator_rows, 'lenslet', axis=0, tiled=True)]
    pallas_call x0 -> x1, Pallas kernels: none -> 40.1 us  [body(): pl.pallas_call(project_kernel, grid_spec=pltpu.PrefetchScalarGridSpec(num...]
    dot_general x1 -> x0, matrix products: 23 us -> none  [body(): jnp.dot(stacked, lax.all_gather(operator_rows, 'lenslet', axis=0, tiled=T...]
    reshape x1 -> x0, local copies, waits for them, and re-layouts: 9.23 us -> none  [body(): table = extended.reshape(depths * rows_ext * cols_ext, pixels)]
    concatenate x1 -> x0, other arithmetic: 8.03 us -> none  [body(): extended = jnp.concatenate([above, volume, below], axis=1)]
    ppermute x2, waiting for transfers between devices: 0.01 us -> 7.35 us  [passed_along(): return lax.ppermute(block, axis, route)]
  transfers between devices with their start and end apart: 3 -> 3, of which waited for: 0 -> 2; matrix products, arithmetic and copies ran while one was open for 77% -> 18% of each run, Pallas kernels for 0% -> 0%
where the time goes in v1:
time: 172 us; the launch traced here: 170 us
  waiting for transfers between devices  63.6 us (37%)
  local copies, waits for them, and re-layouts  43.3 us (25%)
  Pallas kernels  40.1 us (23%)
  between operations  14.1 us (8%)
  starting transfers between devices  6.5 us (4%)
  other arithmetic  2.79 us (2%)
    all_gather x1, waiting for transfers between devices, body(): operators = lax.all_gather(operator_rows, 'lenslet', axis=0, tiled=True)  55.6 us
    pallas_call x1, Pallas kernels, body(): pl.pallas_call(project_kernel, grid_spec=pltpu.PrefetchScalarGridSpec(num...  40.1 us
    unnamed x6, local copies, waits for them, and re-layouts  20.7 us
    all_gather x1, local copies, waits for them, and re-layouts, body(): operators = lax.all_gather(operator_rows, 'lenslet', axis=0, tiled=True)  15.8 us
    ppermute x2, waiting for transfers between devices, passed_along(): return lax.ppermute(block, axis, route)  7.35 us
    ppermute x2, starting transfers between devices, passed_along(): return lax.ppermute(block, axis, route)  6.46 us
    another operation x1, local copies, waits for them, and re-layouts, body(): jnp.stack([extended[:, :, s:s + columns] for s in range(2 * REACH + 1)])  5.49 us
  transfers between devices with their start and end apart: 3, of which 2 were waited for; matrix products, arithmetic and copies ran while one was open for 18% of the time, Pallas kernels for 0%

profile of v1, /device:TPU:1, one launch (start us, length us, event | category | flops | bytes accessed | tf_op | source)
XLA Modules:
  0.0 170.4 jit_solution(15140541964880047693)
XLA Ops:
  7.2 0.0 all-gather.3.cloned.1.call-start
  7.2 0.7 all-gather.3.cloned.1.call-update
  7.9 1.3 fusion
  9.2 4.5 %collective-permute-start = (bf16[4,2,64,400]{3,2,1,0:T(8,128)(2,1)S(1)}, bf16[4,2,64,400]{3,2,1,0:T(8,128)(2,1)S(1)}, u32[]{:S(2)}, u32[]{:S(2)}) collective-permute-start(bf16[4,2,64,400]{3,2,1,0:T(8,128)(2,1)S(1)} %get-tuple-element.7), channel_id=1, source_target_pairs={{0,1},{1,2},{2,3},{3,4},{4,5},{5,6},{6,7},{7,8},{8,9},{9,10},{10,1... | collective-permute-start | bytes 1228808 | tf_op jit(solution)/shard_map/ppermute | solution.py:14
  13.7 1.9 %collective-permute-start.1 = (bf16[4,2,64,400]{3,2,1,0:T(8,128)(2,1)S(1)}, bf16[4,2,64,400]{3,2,1,0:T(8,128)(2,1)S(1)}, u32[]{:S(2)}, u32[]{:S(2)}) collective-permute-start(bf16[4,2,64,400]{3,2,1,0:T(8,128)(2,1)S(1)} %get-tuple-element.6), channel_id=1, source_target_pairs={{1,0},{2,1},{3,2},{4,3},{5,4},{6,5},{7,6},{8,7},{9,8},{10,9},{11,1... | collective-permute-start | bytes 1228808 | tf_op jit(solution)/shard_map/ppermute | solution.py:14
  15.7 0.8 reduce-window.8
  16.5 1.3 add_bitcast_fusion
  17.9 0.6 convert_reduce_fusion.depth_ref
  18.5 7.3 %collective-permute-done = bf16[4,2,64,400]{3,2,1,0:T(8,128)(2,1)S(1)} collective-permute-done((bf16[4,2,64,400]{3,2,1,0:T(8,128)(2,1)S(1)}, bf16[4,2,64,400]{3,2,1,0:T(8,128)(2,1)S(1)}, u32[]{:S(2)}, u32[]{:S(2)}) %collective-permute-start) | collective-permute-done | bytes 409632 | tf_op jit(solution)/shard_map/ppermute | solution.py:14
  25.9 3.0 %constant_dynamic-update-slice_fusion.1 = bf16[4,20,64,400]{3,2,1,0:T(8,128)(2,1)S(1)} fusion(bf16[4,20,64,400]{3,2,1,0:T(8,128)(2,1)S(1)} %constant_dynamic-update-slice_fusion.2, bf16[4,16,64,400]{3,2,1,0:T(8,128)(2,1)} %param.6), kind=kLoop, calls=%fused_computation.6 | loop fusion | bytes 7471104
  28.8 0.0 collective-permute-done.1
  28.9 4.2 %bitcast_dynamic-update-slice_fusion.4 = bf16[5,4,20,64,400]{4,3,2,1,0:T(8,128)(2,1)} fusion(bf16[4,20,64,400]{3,2,1,0:T(8,128)(2,1)S(1)} %constant_dynamic-update-slice_fusion), kind=kLoop, calls=%fused_computation.4 | loop fusion | bytes 9338880
  33.1 5.4 %bitcast_dynamic-update-slice_fusion.3 = bf16[5,4,20,64,400]{4,3,2,1,0:T(8,128)(2,1)} fusion(bf16[5,4,20,64,400]{4,3,2,1,0:T(8,128)(2,1)} %bitcast_dynamic-update-slice_fusion.4, bf16[4,20,64,400]{3,2,1,0:T(8,128)(2,1)S(1)} %constant_dynamic-update-slice_fusion), kind=kLoop, calls=%fused_computation.3 | loop fusion | bytes 9338880
  38.5 2.7 %bitcast_dynamic-update-slice_fusion.2 = bf16[5,4,20,64,400]{4,3,2,1,0:T(8,128)(2,1)} fusion(bf16[5,4,20,64,400]{4,3,2,1,0:T(8,128)(2,1)} %bitcast_dynamic-update-slice_fusion.3, bf16[4,20,64,400]{3,2,1,0:T(8,128)(2,1)S(1)} %constant_dynamic-update-slice_fusion), kind=kLoop, calls=%fused_computation.2 | loop fusion | bytes 9338880
  41.2 5.4 %bitcast_dynamic-update-slice_fusion.1 = bf16[5,4,20,64,400]{4,3,2,1,0:T(8,128)(2,1)} fusion(bf16[5,4,20,64,400]{4,3,2,1,0:T(8,128)(2,1)} %bitcast_dynamic-update-slice_fusion.2, bf16[4,20,64,400]{3,2,1,0:T(8,128)(2,1)S(1)} %constant_dynamic-update-slice_fusion), kind=kLoop, calls=%fused_computation.1 | loop fusion | bytes 9338880
  46.6 5.5 %bitcast_dynamic-update-slice_fusion.vol_ref = bf16[5,4,20,64,400]{4,3,2,1,0:T(8,128)(2,1)} fusion(bf16[5,4,20,64,400]{4,3,2,1,0:T(8,128)(2,1)} %bitcast_dynamic-update-slice_fusion.1, bf16[4,20,64,400]{3,2,1,0:T(8,128)(2,1)S(1)} %constant_dynamic-update-slice_fusion), kind=kLoop, calls=%fused_computation | loop fusion | bytes 9338880 | tf_op jit(solution)/shard_map/stack | solution.py:47
  52.1 55.6 %all-gather.3.cloned.1.call-done = bf16[16,800,400]{1,2,0:T(8,128)(2,1)} async-done(((bf16[1,800,400]{1,2,0:T(8,128)(2,1)}), bf16[16,800,400]{1,2,0:T(8,128)(2,1)}) %all-gather.3.cloned.1.call-update) | async-done | bytes 10240016 | tf_op jit(solution)/shard_map/all_gather | solution.py:48
  107.7 15.8 %copy.10 = bf16[16,800,400]{2,1,0:T(8,128)(2,1)} copy(bf16[16,800,400]{1,2,0:T(8,128)(2,1)} %all-gather.3.cloned.1.call-done) | data formatting | bytes 20480000 | tf_op jit(solution)/shard_map/all_gather | solution.py:48
  123.5 40.1 %shard_map.77 = (f32[1024,400]{1,0:T(8,128)}, f32[1024,400]{1,0:T(8,128)}) custom-call(s32[32]{0:T(128)} %convert_reduce_fusion.depth_ref, s32[32]{0:T(128)} %get-tuple-element.9.row_ref, s32[32]{0:T(128)} %get-tuple-element.8.col_ref, bf16[5,4,20,64,400]{4,3,2,1,0:T(8,128)(2,1)} %bitcast_dynamic-update-slice_fusion.vol_ref, bf16[12800,400]{1,0:T(8,128)(2,1)} %bitcast.22, ...), custom_call_target="tpu_custom_call" | custom-call | tf_op jit(solution)/shard_map/pallas_call | solution.py:51
  (2 shorter events, 0.1 us)
Async XLA Ops:
  7.2 100.5 %all-gather.3.cloned.1.call-start = ((), (), s32[]{:S(2)}) async-start(), calls=%async_computation | async-start | bytes 12185600 | tf_op jit(solution)/shard_map/all_gather | solution.py:48
  9.2 16.6 %collective-permute-start = (bf16[4,2,64,400]{3,2,1,0:T(8,128)(2,1)S(1)}, bf16[4,2,64,400]{3,2,1,0:T(8,128)(2,1)S(1)}, u32[]{:S(2)}, u32[]{:S(2)}) collective-permute-start(bf16[4,2,64,400]{3,2,1,0:T(8,128)(2,1)S(1)} %get-tuple-element.7), channel_id=1, source_target_pairs={{0,1},{1,2},{2,3},{3,4},{4,5},{5,6},{6,7},{7,8},{8,9},{9,10},{10,1... | collective-permute-start | bytes 1228808 | tf_op jit(solution)/shard_map/ppermute | solution.py:14
  13.7 15.1 %collective-permute-start.1 = (bf16[4,2,64,400]{3,2,1,0:T(8,128)(2,1)S(1)}, bf16[4,2,64,400]{3,2,1,0:T(8,128)(2,1)S(1)}, u32[]{:S(2)}, u32[]{:S(2)}) collective-permute-start(bf16[4,2,64,400]{3,2,1,0:T(8,128)(2,1)S(1)} %get-tuple-element.6), channel_id=1, source_target_pairs={{1,0},{2,1},{3,2},{4,3},{5,4},{6,5},{7,6},{8,7},{9,8},{10,9},{11,1... | collective-permute-start | bytes 1228808 | tf_op jit(solution)/shard_map/ppermute | solution.py:14
Sparse Core Ops, SparseCore 0:
  10.2 97.4 all-gather.2
